TPU v7x, 32 devices: a whole 2x2x4 slice. The times are simulated.
32 devices in a mesh: dp: 16 (over z, y, core), head: 2 (over x).
Axes of the slice: x: 2, y: 2, z: 4, core: 2. Of those that a mesh axis runs over, the one named last changes fastest.
Arguments:
- tokens: bfloat16 [2048, 16, 1024], P('head', 'dp'), may hold values from -6 to 6
- lengths: int32 [16], P('dp'), may hold values from 128 to 2048, as said below
- cotangent: bfloat16 [2048, 16, 1024], P('head', 'dp'), may hold values from -6 to 6
- attention_gain: float32 [1024], replicated, may hold values from 0.5 to 1.5
- query_heads: bfloat16 [1024, 96], P(None, 'head'), may hold values from -0.4375 to 0.4375
- key_heads: bfloat16 [1024, 32], P(None, 'head'), may hold values from -0.375 to 0.375
- value_heads: bfloat16 [1024, 32], P(None, 'head'), may hold values from -0.25 to 0.25
- query_basis: bfloat16 [1024, 384], replicated, may hold values from -0.1875 to 0.1875
- key_basis: bfloat16 [1024, 128], replicated, may hold values from -0.1875 to 0.1875
- value_basis: bfloat16 [1024, 128], replicated, may hold values from -0.1875 to 0.1875
- output_weight: bfloat16 [1024, 1024], P('head'), may hold values from -0.75 to 0.75
- feed_gain: float32 [1024], replicated, may hold values from 0.5 to 1.5
- gate_weight: bfloat16 [1024, 2816], P(None, 'head'), may hold values from -0.1875 to 0.1875
- up_weight: bfloat16 [1024, 2816], P(None, 'head'), may hold values from -0.1875 to 0.1875
- down_weight: bfloat16 [2816, 1024], P('head'), may hold values from -0.109375 to 0.109375
Outputs:
- layer_output: bfloat16 [2048, 16, 1024], P('head', 'dp')
- input_grad: float32 [2048, 16, 1024], P('head', 'dp')
- grad_attention_gain: float32 [1024], replicated
- grad_query_heads: float32 [1024, 96], P(None, 'head')
- grad_key_heads: float32 [1024, 32], P(None, 'head')
- grad_value_heads: float32 [1024, 32], P(None, 'head')
- grad_query_basis: float32 [1024, 384], replicated
- grad_key_basis: float32 [1024, 128], replicated
- grad_value_basis: float32 [1024, 128], replicated
- grad_output_weight: float32 [1024, 1024], P('head')
- grad_feed_gain: float32 [1024], replicated
- grad_gate_weight: float32 [1024, 2816], P(None, 'head')
- grad_up_weight: float32 [1024, 2816], P(None, 'head')
- grad_down_weight: float32 [2816, 1024], P('head')
Inputs may be any that keep to these rules, and one draw needn't show every extreme that they name: A sequence's first lengths slots hold its tokens; in every draw some sequence fills all 2048 slots.
All inputs are finite; a program needn't handle non-finite values.
Results may differ from a plain program's by a relative error of at most 0.024.
The roundings to bfloat16 on the way count: a program that leaves them out, or rounds other values in their place, can miss the bound.
Values may be sent and summed in bfloat16 or wider, within the bound.
No kernel may reach another device: no remote copies, remote signals or barrier semaphores. Data moves between devices by JAX's collectives and lax.ppermute only.
A program may use at most 320 MiB of HBM per device.

v0:
```python
import jax
import jax.numpy as jnp
from jax import lax
from jax.sharding import PartitionSpec as P

RQ = 6
RKV = 2


norm_eps = 1e-06
masked_score = -1e30


def rope_tables(slot_count, head_width):
    half_width = head_width // 2
    inverse = jnp.exp(
        jnp.arange(half_width, dtype=jnp.float32)
        * (-2.0 / head_width)
        * jnp.log(jnp.float32(10000.0))
    )
    angles = jnp.arange(slot_count, dtype=jnp.float32)[:, None] * inverse[None, :]
    return (jnp.cos(angles), jnp.sin(angles))


def rotate(factor_basis, cosine_table, sine_table):
    half_width = factor_basis.shape[-1] // 2
    lower_half = factor_basis[..., :half_width]
    upper_half = factor_basis[..., half_width:]
    return jnp.concatenate(
        [
            lower_half * cosine_table - upper_half * sine_table,
            lower_half * sine_table + upper_half * cosine_table,
        ],
        axis=-1,
    )


def unrotate(turned_grad, cosine_table, sine_table):
    half_width = turned_grad.shape[-1] // 2
    lower_half = turned_grad[..., :half_width]
    upper_half = turned_grad[..., half_width:]
    return jnp.concatenate(
        [
            lower_half * cosine_table + upper_half * sine_table,
            upper_half * cosine_table - lower_half * sine_table,
        ],
        axis=-1,
    )


def matmul(first_operand, second_operand):
    return jnp.dot(first_operand, second_operand, preferred_element_type=jnp.float32)


def mix_rank(head_part, turned_part):
    total = head_part[..., 0][..., None] * turned_part[:, :, 0][:, :, None, :]
    for rank_index in range(1, head_part.shape[-1]):
        total = (
            total
            + head_part[..., rank_index][..., None] * turned_part[:, :, rank_index][:, :, None, :]
        )
    return total


def combine(head_part, turned_part, rank):
    return (mix_rank(head_part, turned_part) / rank).astype(jnp.bfloat16)


def factor_grad(grad_rows, turned_part, rank):
    pieces = [
        jnp.sum(grad_rows * turned_part[:, :, rank_index][:, :, None, :], axis=-1)
        for rank_index in range(turned_part.shape[2])
    ]
    return jnp.stack(pieces, axis=-1) / rank


def basis_grad_of(grad_rows, head_part, rank):
    pieces = [
        jnp.sum(grad_rows * head_part[..., rank_index][..., None], axis=2)
        for rank_index in range(head_part.shape[-1])
    ]
    return jnp.stack(pieces, axis=2) / rank


def per_device(
    tokens,
    lengths,
    cotangent,
    attention_gain,
    query_heads,
    key_heads,
    value_heads,
    query_basis,
    key_basis,
    value_basis,
    output_weight,
    feed_gain,
    gate_weight,
    up_weight,
    down_weight,
):
    head_group = lax.axis_size("head")
    part_slots, sequences, model_width = tokens.shape
    all_slots = part_slots * head_group
    local_rows = part_slots * sequences
    full_rows = all_slots * sequences
    head_width = query_basis.shape[1] // RQ
    score_scale = head_width ** (-0.5)
    cosine_all, sine_all = rope_tables(all_slots, head_width)
    basis_cat = jnp.concatenate([query_basis, key_basis, value_basis], axis=1)
    basis_query_cols = RQ * head_width
    basis_pair_cols = RKV * head_width
    positions = jnp.arange(all_slots, dtype=jnp.int32)

    def row_slice(source, row_start, row_count):
        return lax.dynamic_slice_in_dim(source, row_start, row_count, 0)

    def split_heads(head_proj, slot_count, heads_count):
        query_cols = heads_count * RQ
        pair_cols = heads_count * RKV
        head_query = head_proj[:, :query_cols].reshape(slot_count, sequences, heads_count, RQ)
        head_key = head_proj[:, query_cols : query_cols + pair_cols].reshape(
            slot_count, sequences, heads_count, RKV
        )
        head_value = head_proj[:, query_cols + pair_cols :].reshape(
            slot_count, sequences, heads_count, RKV
        )
        return (head_query, head_key, head_value)

    def split_basis(basis_proj, slot_count, cosine_table, sine_table):
        turned_query = rotate(
            basis_proj[:, :basis_query_cols].reshape(slot_count, sequences, RQ, head_width),
            cosine_table,
            sine_table,
        )
        turned_key = rotate(
            basis_proj[:, basis_query_cols : basis_query_cols + basis_pair_cols].reshape(
                slot_count, sequences, RKV, head_width
            ),
            cosine_table,
            sine_table,
        )
        basis_value = basis_proj[:, basis_query_cols + basis_pair_cols :].reshape(
            slot_count, sequences, RKV, head_width
        )
        return (turned_query, turned_key, basis_value)

    def block_mask(block_start, block_rows, length):
        query_pos = block_start + jnp.arange(block_rows, dtype=jnp.int32)
        return (positions[None, :] <= query_pos[:, None]) & (positions[None, :] < length)

    def block_scores(query_block, key_rows, allowed):
        scores = (
            jnp.einsum("qhd,khd->hqk", query_block, key_rows, preferred_element_type=jnp.float32)
            * score_scale
        )
        return jnp.where(allowed[None], scores, masked_score)

    inputs = tokens.reshape(local_rows, model_width).astype(jnp.float32)
    inv_first = lax.rsqrt(jnp.mean(inputs * inputs, axis=-1, keepdims=True) + norm_eps)
    normed = (inputs * inv_first * attention_gain).astype(jnp.bfloat16)
    heads_here = query_heads.shape[1] // RQ
    head_cat = jnp.concatenate([query_heads, key_heads, value_heads], axis=1)
    query_cols = heads_here * RQ
    pair_cols = heads_here * RKV
    cosine_full = cosine_all[:, None, None, :]
    sine_full = sine_all[:, None, None, :]
    normed_full = lax.all_gather(
        normed.reshape(part_slots, sequences, model_width), "head", axis=0, tiled=True
    ).reshape(full_rows, model_width)

    def full_factors():
        head_proj = matmul(normed_full, head_cat)
        basis_proj = matmul(normed_full, basis_cat)
        head_query, head_key, head_value = split_heads(head_proj, all_slots, heads_here)
        turned_query, turned_key, basis_value = split_basis(
            basis_proj, all_slots, cosine_full, sine_full
        )
        return (head_query, head_key, head_value, turned_query, turned_key, basis_value)

    head_query, head_key, head_value, turned_query, turned_key, basis_value = full_factors()
    query_all = combine(head_query, turned_query, RQ)
    key_all = combine(head_key, turned_key, RKV)
    value_all = combine(head_value, basis_value, RKV)
    sequence_index = 0
    query_rows = query_all[:, sequence_index]
    key_rows = key_all[:, sequence_index]
    value_rows = value_all[:, sequence_index]
    length = lengths[sequence_index]
    row_count = query_rows.shape[0]
    heads_count = query_rows.shape[1]
    block_rows = min(512, row_count)
    block_count = row_count // block_rows

    def one_block(block_index):
        block_start = block_index * block_rows
        query_block = row_slice(query_rows, block_start, block_rows)
        scores = block_scores(
            query_block, key_rows, block_mask(0 + block_start, block_rows, length)
        )
        maxima = jnp.max(scores, axis=-1, keepdims=True)
        raised = jnp.exp(scores - maxima)
        totals = jnp.sum(raised, axis=-1, keepdims=True)
        probs_low = (raised / totals).astype(jnp.bfloat16)
        out_block = jnp.einsum(
            "hqk,khd->qhd", probs_low, value_rows, preferred_element_type=jnp.float32
        ).astype(jnp.bfloat16)
        return (out_block, (maxima + jnp.log(totals))[..., 0])

    out_blocks, log_sums = lax.map(one_block, jnp.arange(block_count))
    out_rows, log_sums = (out_blocks.reshape(row_count, heads_count, head_width), log_sums)
    attended = [out_rows]
    log_sum_list = [log_sums]
    mixed_heads = jnp.stack(attended, axis=1).reshape(full_rows, heads_here * head_width)
    attention_out = lax.psum_scatter(
        matmul(
            row_slice(mixed_heads, jnp.int32(0), local_rows * lax.axis_size("head")), output_weight
        ).astype(jnp.bfloat16),
        "head",
        scatter_dimension=0,
        tiled=True,
    ).astype(jnp.float32)
    state = inputs + attention_out
    inv_second = lax.rsqrt(jnp.mean(state * state, axis=-1, keepdims=True) + norm_eps)
    normed_second = (state * inv_second * feed_gain).astype(jnp.bfloat16)
    out_grad = cotangent.reshape(local_rows, model_width)
    feed_rows = lax.all_gather(
        normed_second.reshape(part_slots, sequences, model_width), "head", axis=0, tiled=True
    ).reshape(full_rows, model_width)
    gate_in = matmul(feed_rows, gate_weight)
    up_in = matmul(feed_rows, up_weight)
    sigmoid_gate = jax.nn.sigmoid(gate_in)
    hidden_low = (gate_in * sigmoid_gate * up_in).astype(jnp.bfloat16)
    feed_out = lax.psum_scatter(
        matmul(
            row_slice(hidden_low, jnp.int32(0), local_rows * lax.axis_size("head")), down_weight
        ).astype(jnp.bfloat16),
        "head",
        scatter_dimension=0,
        tiled=True,
    ).astype(jnp.float32)
    layer_output = (
        (state + feed_out).astype(jnp.bfloat16).reshape(part_slots, sequences, model_width)
    )
    out_grad_full = lax.all_gather(cotangent, "head", axis=0, tiled=True).reshape(
        full_rows, model_width
    )
    hidden_grad = matmul(out_grad_full, down_weight.T)
    grad_down = matmul(hidden_low.T, out_grad_full)
    gate_grad = (
        hidden_grad * up_in * sigmoid_gate * (1.0 + gate_in * (1.0 - sigmoid_gate))
    ).astype(jnp.bfloat16)
    up_grad = (hidden_grad * gate_in * sigmoid_gate).astype(jnp.bfloat16)
    grad_gate = matmul(feed_rows.T, gate_grad)
    grad_up = matmul(feed_rows.T, up_grad)
    row_start = jnp.int32(0)
    normed_second_grad = lax.psum_scatter(
        (
            matmul(
                row_slice(gate_grad, row_start, local_rows * lax.axis_size("head")), gate_weight.T
            )
            + matmul(row_slice(up_grad, row_start, local_rows * lax.axis_size("head")), up_weight.T)
        ).astype(jnp.bfloat16),
        "head",
        scatter_dimension=0,
        tiled=True,
    ).astype(jnp.float32)
    scaled_second = feed_gain * normed_second_grad
    gain_second_grad = jnp.sum(normed_second_grad * state * inv_second, axis=0)
    state_grad = (
        out_grad.astype(jnp.float32)
        + inv_second * scaled_second
        - state * inv_second**3 * jnp.mean(scaled_second * state, axis=-1, keepdims=True)
    )
    attention_grad = state_grad.astype(jnp.bfloat16)
    attention_grad_full = lax.all_gather(
        attention_grad.reshape(part_slots, sequences, model_width), "head", axis=0, tiled=True
    ).reshape(full_rows, model_width)
    grad_output = matmul(mixed_heads.T, attention_grad_full)
    heads_grad = (
        matmul(attention_grad_full, output_weight.T)
        .astype(jnp.bfloat16)
        .reshape(all_slots, sequences, heads_here, head_width)
    )
    head_query, head_key, head_value, turned_query, turned_key, basis_value = full_factors()
    query_all = combine(head_query, turned_query, RQ)
    key_all = combine(head_key, turned_key, RKV)
    value_all = combine(head_value, basis_value, RKV)
    sequence_index = 0
    attend_query_rows = query_all[:, sequence_index]
    attend_key_rows = key_all[:, sequence_index]
    attend_value_rows = value_all[:, sequence_index]
    grad_rows = heads_grad[:, sequence_index]
    log_sums = log_sum_list[sequence_index]
    attend_length = lengths[sequence_index]
    row_count = attend_query_rows.shape[0]
    heads_count = attend_query_rows.shape[1]
    attend_block_rows = min(512, row_count)
    block_count = row_count // attend_block_rows

    def one_block(carried, block_index):
        key_grad, value_grad = carried
        block_start = block_index * attend_block_rows
        query_block = row_slice(attend_query_rows, block_start, attend_block_rows)
        grad_block = row_slice(grad_rows, block_start, attend_block_rows)
        allowed = block_mask(0 + block_start, attend_block_rows, attend_length)
        scores = block_scores(query_block, attend_key_rows, allowed)
        probabilities = jnp.where(
            allowed[None], jnp.exp(scores - log_sums[block_index][..., None]), 0.0
        )
        prob_grad = jnp.einsum(
            "qhd,khd->hqk", grad_block, attend_value_rows, preferred_element_type=jnp.float32
        )
        centre = jnp.sum(probabilities * prob_grad, axis=-1, keepdims=True)
        score_grad = (probabilities * (prob_grad - centre)).astype(jnp.bfloat16)
        query_grad = (
            jnp.einsum(
                "hqk,khd->qhd", score_grad, attend_key_rows, preferred_element_type=jnp.float32
            )
            * score_scale
        ).astype(jnp.bfloat16)
        key_grad = (
            key_grad
            + jnp.einsum(
                "hqk,qhd->khd", score_grad, query_block, preferred_element_type=jnp.float32
            )
            * score_scale
        )
        value_grad = value_grad + jnp.einsum(
            "hqk,qhd->khd",
            probabilities.astype(jnp.bfloat16),
            grad_block,
            preferred_element_type=jnp.float32,
        )
        return ((key_grad, value_grad), query_grad)

    zero_block = jnp.zeros(attend_key_rows.shape, jnp.float32)
    (key_grad, value_grad), query_blocks = lax.scan(
        one_block, (zero_block, zero_block), jnp.arange(block_count)
    )
    query_grad, key_grad, value_grad = (
        query_blocks.reshape(row_count, heads_count, head_width),
        key_grad,
        value_grad,
    )
    query_grads = [query_grad]
    key_grads = [key_grad]
    value_grads = [value_grad]
    query_grad_all = jnp.stack(query_grads, axis=1).astype(jnp.float32)
    key_grad_all = jnp.stack(key_grads, axis=1)
    value_grad_all = jnp.stack(value_grads, axis=1)
    head_query_grad = factor_grad(query_grad_all, turned_query, RQ).astype(jnp.bfloat16)
    head_key_grad = factor_grad(key_grad_all, turned_key, RKV).astype(jnp.bfloat16)
    head_value_grad = factor_grad(value_grad_all, basis_value, RKV).astype(jnp.bfloat16)
    turned_query_grad = basis_grad_of(query_grad_all, head_query, RQ)
    turned_key_grad = basis_grad_of(key_grad_all, head_key, RKV)
    basis_value_grad = basis_grad_of(value_grad_all, head_value, RKV)
    head_grad_cat = jnp.concatenate(
        [
            head_query_grad.reshape(full_rows, query_cols),
            head_key_grad.reshape(full_rows, pair_cols),
            head_value_grad.reshape(full_rows, pair_cols),
        ],
        axis=1,
    )
    basis_grad_cat = jnp.concatenate(
        [
            unrotate(turned_query_grad, cosine_full, sine_full).reshape(
                full_rows, basis_query_cols
            ),
            unrotate(turned_key_grad, cosine_full, sine_full).reshape(full_rows, basis_pair_cols),
            basis_value_grad.reshape(full_rows, basis_pair_cols),
        ],
        axis=1,
    )
    grad_heads = matmul(normed_full.T, head_grad_cat)
    grad_query_part = grad_heads[:, :query_cols]
    grad_key_part = grad_heads[:, query_cols : query_cols + pair_cols]
    grad_value_part = grad_heads[:, query_cols + pair_cols :]
    row_start = jnp.int32(0)
    head_part = row_slice(head_grad_cat, row_start, local_rows * lax.axis_size("head"))
    basis_part = row_slice(basis_grad_cat, row_start, local_rows * lax.axis_size("head"))
    back_slice = lax.psum_scatter(
        jnp.concatenate([matmul(head_part, head_cat.T), basis_part], axis=1).astype(jnp.bfloat16),
        "head",
        scatter_dimension=0,
        tiled=True,
    ).astype(jnp.float32)
    basis_grad_low = back_slice[:, model_width:].astype(jnp.bfloat16)
    normed_grad = back_slice[:, :model_width] + matmul(basis_grad_low, basis_cat.T)
    grad_basis = matmul(normed.T, basis_grad_low)
    scaled_first = attention_gain * normed_grad
    gain_first_grad = jnp.sum(normed_grad * inputs * inv_first, axis=0)
    input_grad = (
        state_grad
        + inv_first * scaled_first
        - inputs * inv_first**3 * jnp.mean(scaled_first * inputs, axis=-1, keepdims=True)
    )
    summed_heads = (
        lax.psum(grad_query_part.astype(jnp.bfloat16), "dp").astype(jnp.float32),
        lax.psum(grad_key_part.astype(jnp.bfloat16), "dp").astype(jnp.float32),
        lax.psum(grad_value_part.astype(jnp.bfloat16), "dp").astype(jnp.float32),
        lax.psum(grad_output.astype(jnp.bfloat16), "dp").astype(jnp.float32),
        lax.psum(grad_gate.astype(jnp.bfloat16), "dp").astype(jnp.float32),
        lax.psum(grad_up.astype(jnp.bfloat16), "dp").astype(jnp.float32),
        lax.psum(grad_down.astype(jnp.bfloat16), "dp").astype(jnp.float32),
    )
    summed_shared = lax.psum(
        (
            grad_basis[:, :basis_query_cols],
            grad_basis[:, basis_query_cols : basis_query_cols + basis_pair_cols],
            grad_basis[:, basis_query_cols + basis_pair_cols :],
            gain_first_grad,
            gain_second_grad,
        ),
        ("dp", "head"),
    )
    return (
        layer_output,
        input_grad.reshape(part_slots, sequences, model_width),
        summed_shared[3],
        summed_heads[0],
        summed_heads[1],
        summed_heads[2],
        summed_shared[0],
        summed_shared[1],
        summed_shared[2],
        summed_heads[3],
        summed_shared[4],
        summed_heads[4],
        summed_heads[5],
        summed_heads[6],
    )


def solution(mesh):
    in_specs = (
        P("head", "dp", None),
        P("dp"),
        P("head", "dp", None),
        P(),
        P(None, "head"),
        P(None, "head"),
        P(None, "head"),
        P(),
        P(),
        P(),
        P("head", None),
        P(),
        P(None, "head"),
        P(None, "head"),
        P("head", None),
    )
    out_specs = (
        P("head", "dp", None),
        P("head", "dp", None),
        P(),
        P(None, "head"),
        P(None, "head"),
        P(None, "head"),
        P(),
        P(),
        P(),
        P("head", None),
        P(),
        P(None, "head"),
        P(None, "head"),
        P("head", None),
    )
    return jax.shard_map(
        per_device, mesh=mesh, in_specs=in_specs, out_specs=out_specs, check_vma=False
    )
```

profile of v0, /device:TPU:0, one launch (start us, length us, event | category | flops | bytes accessed | tf_op | source)
XLA Modules:
  0.0 1716.7 jit_solution(8642102143645440982)
XLA Ops:
  21.5 52.3 %all-gather.7.cloned.1.call-done = bf16[2048,1,1024]{2,0,1:T(8,128)(2,1)} async-done(((bf16[1024,1,1024]{2,0,1:T(8,128)(2,1)}), bf16[2048,1,1024]{2,0,1:T(8,128)(2,1)}) %all-gather.7.cloned.1.call-update) | async-done | bytes 4194320 | tf_op jit(solution)/shard_map/all_gather | solution.py:168
  105.9 196.2 %while.30 = (s32[]{:T(128)}, bf16[4,512,8,64]{1,3,2,0:T(8,128)(2,1)}, f32[4,8,512]{2,1,0:T(8,128)}, s32[4]{0:T(128)S(1)}, s32[]{:T(128)}, /*index=5*/bf16[2048,8...) while((s32[]{:T(128)}, ...), condition=%wide.region_4.5_spmd.clone.clone, body=%wide.region_1.4_spmd.clone.clone.sunk | while | flops 2260990464 | bytes 110502168 | solution.py:210
  108.5 15.1 fusion.199
  138.7 15.5 fusion.201
  187.7 15.5 fusion.201
  236.7 15.5 fusion.201
  285.7 15.5 fusion.201
  311.8 54.5 %reduce-scatter.5.cloned.1.call-done = bf16[1024,1024]{1,0:T(8,128)(2,1)} async-done(((bf16[2048,1024]{1,0:T(8,128)(2,1)}), bf16[1024,1024]{1,0:T(8,128)(2,1)}) %reduce-scatter.5.cloned.1.call-update) | async-done | bytes 2097168 | tf_op jit(solution)/shard_map/reduce_scatter | solution.py:215
  372.5 56.3 %all-gather.11.cloned.1.call-done = bf16[2048,1024]{1,0:T(8,128)(2,1)} async-done(((bf16[1024,1024]{1,0:T(8,128)(2,1)}), bf16[2048,1024]{1,0:T(8,128)(2,1)}) %all-gather.11.cloned.1.call-update) | async-done | bytes 4194320 | tf_op jit(solution)/shard_map/all_gather | solution.py:227
  450.6 36.3 %all-gather.9.cloned.1.call-done = bf16[2048,1,1024]{2,0,1:T(8,128)(2,1)} async-done(((bf16[1024,1,1024]{2,0,1:T(8,128)(2,1)}), bf16[2048,1,1024]{2,0,1:T(8,128)(2,1)}) %all-gather.9.cloned.1.call-update) | async-done | bytes 4194320 | tf_op jit(solution)/shard_map/all_gather | solution.py:245
  486.9 20.5 %multiply_convert_fusion.24 = (bf16[2048,1408]{1,0:T(8,128)(2,1)}, bf16[2048,1408]{1,0:T(8,128)(2,1)}, bf16[2048,1408]{1,0:T(8,128)(2,1)}) fusion(f32[2048,1408]{1,0:T(8,128)} %fusion.152, f32[2048,1408]{1,0:T(8,128)} %fusion.153, bf16[1408,1024]{1,0:T(8,128)(2,1)S(1)} %copy-done, bf16[2048,1,1024]{2,0,1:T(8,128)(2,1)} %all-gather.9.cloned.1.call-done), kind=kOutput, calls=%fused_computation.97 | convolution fusion | flops 5951717376 | bytes 47448064 | tf_op jit(solution)/shard_map/dot_general | solution.py:52
  549.1 31.2 %reduce-scatter.9.cloned.1.call-done = bf16[1024,1024]{1,0:T(8,128)(2,1)} async-done(((bf16[2048,1024]{1,0:T(8,128)(2,1)}), bf16[1024,1024]{1,0:T(8,128)(2,1)}) %reduce-scatter.9.cloned.1.call-update) | async-done | bytes 2097168 | tf_op jit(solution)/shard_map/reduce_scatter | solution.py:257
  620.7 26.4 %all-gather.13.cloned.1.call-done = bf16[2048,1024]{1,0:T(8,128)(2,1)} async-done(((bf16[1024,1024]{1,0:T(8,128)(2,1)}), bf16[2048,1024]{1,0:T(8,128)(2,1)}) %all-gather.13.cloned.1.call-update) | async-done | bytes 4194320 | tf_op jit(solution)/shard_map/all_gather | solution.py:276
  654.8 449.4 %while.31 = (s32[]{:T(128)}, f32[2048,8,64]{0,2,1:T(8,128)}, f32[2048,8,64]{0,2,1:T(8,128)}, bf16[4,512,8,64]{1,3,2,0:T(8,128)(2,1)}, s32[4]{0:T(128)S(1)}, /*in...) while((s32[]{:T(128)}, f32[2048,8,64]{0,2,1:T(8,128)}, ...), condition=%wide.region_12.13_spmd.clone.clone, body=%wide.region_10.12_spmd.clone.clone.sunk | while | flops 5476186624 | bytes 315056768 | solution.py:338
  675.2 26.7 %multiply_reduce_fusion.11 = (f32[8,512]{1,0:T(8,128)S(1)}, f32[8,512,2048]{2,1,0:T(8,128)}) fusion(f32[8,512,2048]{2,1,0:T(8,128)} %fusion.208, f32[8,512]{1,0:T(8,128)S(1)} %dynamic-slice_bitcast_fusion.2, f32[2048,64]{0,1:T(8,128)S(1)} %copy-done.34, f32[2048,8]{0,1:T(8,128)S(1)} %copy-done.38, f32[2048,64]{0,1:T(8,128)S(1)} %copy-done.33, ...), kind=kOutput, calls=%fused_computation.40.clone.1 | convolution fusion | flops 1129312256 | bytes 69894144 | tf_op jit(solution)/shard_map/while/body/eval_jaxpr/qhd,khd->hqk/dot_general | solution.py:154
  701.9 27.5 %multiply_convert_fusion.37 = bf16[8,512,2048]{2,1,0:T(8,128)(2,1)} fusion(f32[8,512,2048]{2,1,0:T(8,128)} %get-tuple-element.713, f32[8,512,2048]{2,1,0:T(8,128)} %fusion.208, f32[8,512]{1,0:T(8,128)S(1)} %get-tuple-element.714), kind=kLoop, calls=%fused_computation.39.clone.1 | loop fusion | flops 25165824 | bytes 83902464 | tf_op jit(solution)/shard_map/while/body/eval_jaxpr/convert_element_type | solution.py:315
  729.4 15.7 bitcast_add_fusion.5
  786.5 26.7 %multiply_reduce_fusion.11 = (f32[8,512]{1,0:T(8,128)S(1)}, f32[8,512,2048]{2,1,0:T(8,128)}) fusion(f32[8,512,2048]{2,1,0:T(8,128)} %fusion.208, f32[8,512]{1,0:T(8,128)S(1)} %dynamic-slice_bitcast_fusion.2, f32[2048,64]{0,1:T(8,128)S(1)} %copy-done.34, f32[2048,8]{0,1:T(8,128)S(1)} %copy-done.38, f32[2048,64]{0,1:T(8,128)S(1)} %copy-done.33, ...), kind=kOutput, calls=%fused_computation.40.clone.1 | convolution fusion | flops 1129312256 | bytes 69894144 | tf_op jit(solution)/shard_map/while/body/eval_jaxpr/qhd,khd->hqk/dot_general | solution.py:154
  813.2 27.5 %multiply_convert_fusion.37 = bf16[8,512,2048]{2,1,0:T(8,128)(2,1)} fusion(f32[8,512,2048]{2,1,0:T(8,128)} %get-tuple-element.713, f32[8,512,2048]{2,1,0:T(8,128)} %fusion.208, f32[8,512]{1,0:T(8,128)S(1)} %get-tuple-element.714), kind=kLoop, calls=%fused_computation.39.clone.1 | loop fusion | flops 25165824 | bytes 83902464 | tf_op jit(solution)/shard_map/while/body/eval_jaxpr/convert_element_type | solution.py:315
  840.6 17.0 bitcast_add_fusion.5
  899.0 26.7 %multiply_reduce_fusion.11 = (f32[8,512]{1,0:T(8,128)S(1)}, f32[8,512,2048]{2,1,0:T(8,128)}) fusion(f32[8,512,2048]{2,1,0:T(8,128)} %fusion.208, f32[8,512]{1,0:T(8,128)S(1)} %dynamic-slice_bitcast_fusion.2, f32[2048,64]{0,1:T(8,128)S(1)} %copy-done.34, f32[2048,8]{0,1:T(8,128)S(1)} %copy-done.38, f32[2048,64]{0,1:T(8,128)S(1)} %copy-done.33, ...), kind=kOutput, calls=%fused_computation.40.clone.1 | convolution fusion | flops 1129312256 | bytes 69894144 | tf_op jit(solution)/shard_map/while/body/eval_jaxpr/qhd,khd->hqk/dot_general | solution.py:154
  925.7 27.5 %multiply_convert_fusion.37 = bf16[8,512,2048]{2,1,0:T(8,128)(2,1)} fusion(f32[8,512,2048]{2,1,0:T(8,128)} %get-tuple-element.713, f32[8,512,2048]{2,1,0:T(8,128)} %fusion.208, f32[8,512]{1,0:T(8,128)S(1)} %get-tuple-element.714), kind=kLoop, calls=%fused_computation.39.clone.1 | loop fusion | flops 25165824 | bytes 83902464 | tf_op jit(solution)/shard_map/while/body/eval_jaxpr/convert_element_type | solution.py:315
  953.2 16.9 bitcast_add_fusion.5
  1011.5 26.7 %multiply_reduce_fusion.11 = (f32[8,512]{1,0:T(8,128)S(1)}, f32[8,512,2048]{2,1,0:T(8,128)}) fusion(f32[8,512,2048]{2,1,0:T(8,128)} %fusion.208, f32[8,512]{1,0:T(8,128)S(1)} %dynamic-slice_bitcast_fusion.2, f32[2048,64]{0,1:T(8,128)S(1)} %copy-done.34, f32[2048,8]{0,1:T(8,128)S(1)} %copy-done.38, f32[2048,64]{0,1:T(8,128)S(1)} %copy-done.33, ...), kind=kOutput, calls=%fused_computation.40.clone.1 | convolution fusion | flops 1129312256 | bytes 69894144 | tf_op jit(solution)/shard_map/while/body/eval_jaxpr/qhd,khd->hqk/dot_general | solution.py:154
  1038.2 27.5 %multiply_convert_fusion.37 = bf16[8,512,2048]{2,1,0:T(8,128)(2,1)} fusion(f32[8,512,2048]{2,1,0:T(8,128)} %get-tuple-element.713, f32[8,512,2048]{2,1,0:T(8,128)} %fusion.208, f32[8,512]{1,0:T(8,128)S(1)} %get-tuple-element.714), kind=kLoop, calls=%fused_computation.39.clone.1 | loop fusion | flops 25165824 | bytes 83902464 | tf_op jit(solution)/shard_map/while/body/eval_jaxpr/convert_element_type | solution.py:315
  1065.7 16.9 bitcast_add_fusion.5
  1203.4 17.0 all-reduce.10.cloned.1.call-done
  1223.2 195.1 %all-reduce.12.cloned.1.call-done = (bf16[1024,48]{0,1:T(8,128)(2,1)}, bf16[512,1024]{1,0:T(8,128)(2,1)}, bf16[1024,1408]{1,0:T(8,128)(2,1)}, bf16[1024,1408]{1,0:T(8,128)(2,1)}, bf16[1408,1024]{1,0:T(8,128)(2,1)}) async-done(((bf16[1024,48]{0,1:T(8,128)(2,1)}, bf16[512,1024]{1,0:T(8,128)(2,1)}, bf16[1024,1408]{1,0:T(8,128)(2,1)}, bf16[1024,1408]{1,0:T(8,128)(2,1)}, bf16[1408,1024]{1,0:T(8,128)(2,1)}), ...) | async-done | bytes 9797648 | tf_op jit(solution)/shard_map/psum | solution.py:400
  1432.9 70.5 %reduce-scatter.11.cloned.1.call-done = bf16[1024,1664]{1,0:T(8,128)(2,1)} async-done(((bf16[2048,1664]{1,0:T(8,128)(2,1)}), bf16[1024,1664]{1,0:T(8,128)(2,1)}) %reduce-scatter.11.cloned.1.call-update) | async-done | bytes 3407888 | tf_op jit(solution)/shard_map/reduce_scatter | solution.py:383
  1517.9 42.1 %reduce-scatter.7.cloned.1.call-done = bf16[1024,1024]{1,0:T(8,128)(2,1)} async-done(((bf16[2048,1024]{1,0:T(8,128)(2,1)}), bf16[1024,1024]{1,0:T(8,128)(2,1)}) %reduce-scatter.7.cloned.1.call-update) | async-done | bytes 2097168 | tf_op jit(solution)/shard_map/reduce_scatter | solution.py:234
  1577.3 39.5 %all-reduce = (f32[1024]{0:T(1024)}, f32[1024]{0:T(1024)}) all-reduce(f32[1024]{0:T(1024)S(1)} %get-tuple-element.353, f32[1024]{0:T(1024)S(1)} %copy-done.59), channel_id=1, replica_groups=mesh['dp'=16,'head'=2] {'dp','head'}, use_global_device_ids=true, to_apply=%region_36.37 | all-reduce | flops 2048 | bytes 16384 | tf_op jit(solution)/shard_map/psum | solution.py:408
  1616.8 87.6 %all-reduce.8.cloned.1.call-done = (f32[1024,384]{1,0:T(8,128)}, f32[1024,128]{1,0:T(8,128)}, f32[1024,128]{1,0:T(8,128)}) async-done(((f32[1024,384]{1,0:T(8,128)}, f32[1024,128]{1,0:T(8,128)}, f32[1024,128]{1,0:T(8,128)}), (f32[1024,384]{1,0:T(8,128)}, f32[1024,128]{1,0:T(8,128)}, f32[1024,128]{1,0:T(8,128)})) %all-reduce.8.cloned.1.call-update) | async-done | bytes 2621456 | tf_op jit(solution)/shard_map/psum | solution.py:408
  (423 shorter events, 596.9 us)
Async XLA Ops:
  7.2 479.8 %copy-start = (bf16[1408,1024]{1,0:T(8,128)(2,1)S(1)}, bf16[1408,1024]{1,0:T(8,128)(2,1)}, u32[]{:S(2)}) copy-start(bf16[1408,1024]{1,0:T(8,128)(2,1)} %param.33) | copy-start | bytes 8650756
  7.2 66.6 %all-gather.7.cloned.1.call-start = ((), (), s32[]{:S(2)}) async-start(), calls=%async_computation.4 | async-start | bytes 6291456 | tf_op jit(solution)/shard_map/all_gather | solution.py:168
  14.2 352.1 %reduce-scatter.5.cloned.1.call-start = ((), (), s32[]{:S(2)}) async-start(), calls=%async_computation.5 | async-start | bytes 6291456 | tf_op jit(solution)/shard_map/reduce_scatter | solution.py:215
  21.5 76.3 %copy-start.11 = (f32[2048,32]{0,1:T(8,128)}, f32[2048,32]{0,1:T(8,128)S(1)}, u32[]{:S(2)}) copy-start(f32[2048,32]{0,1:T(8,128)S(1)} %get-tuple-element.504) | copy-start | bytes 786436
  21.5 76.3 %copy-start.13 = (f32[2048,32]{0,1:T(8,128)}, f32[2048,32]{0,1:T(8,128)S(1)}, u32[]{:S(2)}) copy-start(f32[2048,32]{0,1:T(8,128)S(1)} %get-tuple-element.505) | copy-start | bytes 786436
  123.6 15.1 copy-start.5
  172.6 15.1 copy-start.5
  221.6 15.1 copy-start.5
  270.6 15.1 copy-start.5
  311.8 57.7 %copy-start.49 = (f32[1024]{0:T(1024)S(1)}, f32[1024]{0:T(1024)}, u32[]{:S(2)}) copy-start(f32[1024]{0:T(1024)} %param.30) | copy-start | bytes 12292
  311.8 117.0 %all-gather.11.cloned.1.call-start = ((), (), s32[]{:S(2)}) async-start(), calls=%async_computation.10 | async-start | bytes 6291456 | tf_op jit(solution)/shard_map/all_gather | solution.py:227
  369.5 216.2 %copy-start.46 = (f32[1024]{0:T(1024)}, f32[1024]{0:T(1024)S(1)}, u32[]{:S(2)}) copy-start(f32[1024]{0:T(1024)S(1)} %get-tuple-element.503) | copy-start | bytes 12292
  369.5 216.1 %copy-start.51 = (f32[1024]{0:T(1024)}, f32[1024]{0:T(1024)S(1)}, u32[]{:S(2)}) copy-start(f32[1024]{0:T(1024)S(1)} %get-tuple-element.502) | copy-start | bytes 12292
  371.9 115.0 %all-gather.9.cloned.1.call-start = ((), (), s32[]{:S(2)}) async-start(), calls=%async_computation.7 | async-start | bytes 6291456 | tf_op jit(solution)/shard_map/all_gather | solution.py:245
  372.5 207.8 %reduce-scatter.9.cloned.1.call-start = ((), (), s32[]{:S(2)}) async-start(), calls=%async_computation.8 | async-start | bytes 6291456 | tf_op jit(solution)/shard_map/reduce_scatter | solution.py:257
  525.8 121.3 %all-gather.13.cloned.1.call-start = ((), (), s32[]{:S(2)}) async-start(), calls=%async_computation.11 | async-start | bytes 6291456 | tf_op jit(solution)/shard_map/all_gather | solution.py:276
  590.2 630.2 %all-reduce.10.cloned.1.call-start = ((), (), s32[]{:S(2)}) async-start(), calls=%async_computation.13 | async-start | bytes 131072 | tf_op jit(solution)/shard_map/psum | solution.py:401
  590.3 22.9 %slice-start.1 = ((s8[5767168]{0:T(1024)(128)(4,1)}), s8[4194304]{0:T(1024)(128)(4,1)S(1)}, s32[]{:S(2)}) async-start(s8[5767168]{0:T(1024)(128)(4,1)} %bitcast.303), calls=%async_computation.16 | async-start | bytes 8388608
  660.8 14.4 copy-start.33
  1133.9 284.4 %all-reduce.12.cloned.1.call-start = ((), (), s32[]{:S(2)}) async-start(), calls=%async_computation.14 | async-start | bytes 19595264 | tf_op jit(solution)/shard_map/psum | solution.py:400
  1140.8 362.6 %reduce-scatter.11.cloned.1.call-start = ((), (), s32[]{:S(2)}) async-start(), calls=%async_computation.9 | async-start | bytes 10223616 | tf_op jit(solution)/shard_map/reduce_scatter | solution.py:383
  1151.0 17.6 %copy-start.12 = (f32[2048,32]{0,1:T(8,128)S(1)}, f32[2048,32]{0,1:T(8,128)}, u32[]{:S(2)}) copy-start(f32[2048,32]{0,1:T(8,128)} %copy-done.11) | copy-start | bytes 786436
  1151.0 17.6 %copy-start.14 = (f32[2048,32]{0,1:T(8,128)S(1)}, f32[2048,32]{0,1:T(8,128)}, u32[]{:S(2)}) copy-start(f32[2048,32]{0,1:T(8,128)} %copy-done.13) | copy-start | bytes 786436
  1192.0 368.0 %reduce-scatter.7.cloned.1.call-start = ((), (), s32[]{:S(2)}) async-start(), calls=%async_computation.6 | async-start | bytes 6291456 | tf_op jit(solution)/shard_map/reduce_scatter | solution.py:234
  1203.1 501.3 %all-reduce.8.cloned.1.call-start = ((), (), s32[]{:S(2)}) async-start(), calls=%async_computation.12 | async-start | bytes 5242880 | tf_op jit(solution)/shard_map/psum | solution.py:408
  1429.6 73.8 %copy-start.56 = (f32[1024]{0:T(1024)S(1)}, f32[1024]{0:T(1024)}, u32[]{:S(2)}) copy-start(f32[1024]{0:T(1024)} %copy-done.55) | copy-start | bytes 12292
  1429.6 73.8 %copy-start.60 = (f32[1024]{0:T(1024)S(1)}, f32[1024]{0:T(1024)}, u32[]{:S(2)}) copy-start(f32[1024]{0:T(1024)} %param.22) | copy-start | bytes 12292
  1509.7 50.3 %copy-start.47 = (f32[1024]{0:T(1024)S(1)}, f32[1024]{0:T(1024)}, u32[]{:S(2)}) copy-start(f32[1024]{0:T(1024)} %copy-done.46) | copy-start | bytes 12292
  1509.7 50.3 %copy-start.50 = (f32[1024]{0:T(1024)S(1)}, f32[1024]{0:T(1024)}, u32[]{:S(2)}) copy-start(f32[1024]{0:T(1024)} %param.30) | copy-start | bytes 12292
  1509.8 50.2 %copy-start.52 = (f32[1024]{0:T(1024)S(1)}, f32[1024]{0:T(1024)}, u32[]{:S(2)}) copy-start(f32[1024]{0:T(1024)} %copy-done.51) | copy-start | bytes 12292
  1509.8 50.2 %copy-start.54 = (f32[1024]{0:T(1024)S(1)}, f32[1024]{0:T(1024)}, u32[]{:S(2)}) copy-start(f32[1024]{0:T(1024)} %copy-done.53) | copy-start | bytes 12292
  1509.8 50.2 %copy-start.58 = (f32[1024]{0:T(1024)S(1)}, f32[1024]{0:T(1024)}, u32[]{:S(2)}) copy-start(f32[1024]{0:T(1024)} %get-tuple-element.500) | copy-start | bytes 12292
  (79 other events, 592.2 us)
Sparse Core Ops, SparseCore 0:
  14.3 59.4 all-gather.6
  311.9 54.3 reduce-scatter.4
  372.0 56.7 all-gather.10
  430.2 56.7 all-gather.8
  525.9 54.3 reduce-scatter.8
  590.3 56.7 all-gather.12
  1134.0 86.3 all-reduce.9
  1225.9 192.3 all-reduce.11
  1420.6 82.8 reduce-scatter.10
  1505.6 54.3 reduce-scatter.6
  1566.9 137.4 all-reduce.7
where the time goes:
time: 1730 us; the launch traced here: 1720 us
  waiting for transfers between devices  670 us (39%)
  matrix products  575 us (33%)
  other arithmetic  267 us (15%)
  local copies, waits for them, and re-layouts  134 us (8%)
  blocking collectives  39.5 us (2%)
    psum x1, waiting for transfers between devices, per_device(): lax.psum(grad_query_part.astype(jnp.bfloat16), 'dp').astype(jnp.float32)  195 us
    dot_general x8, matrix products, block_scores(): jnp.einsum('qhd,khd->hqk', query_block, key_rows, preferred_element_type=...  167 us
    dot_general x18, matrix products, matmul(): jnp.dot(first_operand, second_operand, preferred_element_type=jnp.float32)  144 us
    convert_element_type x4, other arithmetic, one_block(): score_grad = (probabilities * (prob_grad - centre)).astype(jnp.bfloat16)  110 us
    psum x1, waiting for transfers between devices, per_device(): lax.psum((grad_basis[:, :basis_query_cols], grad_basis[:, basis_query_col...  87.6 us
    reduce_scatter x1, waiting for transfers between devices, per_device(): lax.psum_scatter(jnp.concatenate([matmul(head_part, head_cat.T), basis_pa...  70.5 us
    dot_general x4, matrix products, one_block(): jnp.einsum('hqk,qhd->khd', probabilities.astype(jnp.bfloat16), grad_block...  66.6 us
    dot_general x4, matrix products, one_block(): jnp.einsum('hqk,khd->qhd', probs_low, value_rows, preferred_element_type=...  62.2 us
  transfers between devices with their start and end apart: 11, of which 11 were waited for; matrix products, arithmetic and copies ran while one was open for 12% of the time, Pallas kernels for 0%

commit v1 on v0

--- a/solution.py
+++ b/solution.py
@@ -2,6 +2,162 @@
 import jax.numpy as jnp
 from jax import lax
 from jax.sharding import PartitionSpec as P
+from jax.experimental import pallas as pl
+from jax.experimental.pallas import tpu as pltpu
+import functools
+
+MASKED = -1e30
+
+
+def _mask(s, row0, col0, length):
+    rows = row0 + lax.broadcasted_iota(jnp.int32, s.shape, 0)
+    cols = col0 + lax.broadcasted_iota(jnp.int32, s.shape, 1)
+    allowed = (cols <= rows) & (cols < length)
+    return jnp.where(allowed, s, MASKED)
+
+
+def _fwd_kernel(len_ref, q_ref, k_ref, v_ref, o_ref, of_ref, m_ref, il_ref, s_scr, *, tq, tk, scale):
+    qb = pl.program_id(1)
+    length = len_ref[0]
+    n_kb = jnp.minimum((qb * tq + tq + tk - 1) // tk, (length + tk - 1) // tk)
+    q = q_ref[0]
+
+    def pass_one(kb, carry):
+        m, l = carry
+        k = k_ref[0, pl.ds(pl.multiple_of(kb * tk, tk), tk), :]
+        s = lax.dot_general(q, k, (((1,), (1,)), ((), ())), preferred_element_type=jnp.float32) * scale
+        s = _mask(s, qb * tq, kb * tk, length)
+        s_scr[kb] = s
+        m_new = jnp.maximum(m, jnp.max(s, axis=1, keepdims=True))
+        l = l * jnp.exp(m - m_new) + jnp.sum(jnp.exp(s - m_new), axis=1, keepdims=True)
+        return m_new, l
+
+    m0 = jnp.full((tq, 1), -jnp.inf, jnp.float32)
+    l0 = jnp.zeros((tq, 1), jnp.float32)
+    m, l = lax.fori_loop(0, n_kb, pass_one, (m0, l0))
+    inv_l = 1.0 / l
+
+    def pass_two(kb, carry):
+        acc, low = carry
+        p = jnp.exp(s_scr[kb] - m) * inv_l
+        p_high = p.astype(jnp.bfloat16)
+        p_low = (p - p_high.astype(jnp.float32)).astype(jnp.bfloat16)
+        v = v_ref[0, pl.ds(pl.multiple_of(kb * tk, tk), tk), :]
+        acc = acc + jnp.dot(p_high, v, preferred_element_type=jnp.float32)
+        low = low + jnp.dot(p_low, v, preferred_element_type=jnp.float32)
+        return acc, low
+
+    zero = jnp.zeros(o_ref.shape[1:], jnp.float32)
+    acc, low = lax.fori_loop(0, n_kb, pass_two, (zero, zero))
+    o_ref[0] = acc.astype(o_ref.dtype)
+    of_ref[0] = acc + low
+    m_ref[0] = m
+    il_ref[0] = inv_l
+
+
+def attention_fwd(q, k, v, length, *, tq=256, tk=256):
+    heads, slots, width = q.shape
+    nq = slots // tq
+    kernel = functools.partial(_fwd_kernel, tq=tq, tk=tk, scale=width ** (-0.5))
+    return pl.pallas_call(
+        kernel,
+        out_shape=(
+            jax.ShapeDtypeStruct((heads, slots, width), jnp.bfloat16),
+            jax.ShapeDtypeStruct((heads, slots, width), jnp.float32),
+            jax.ShapeDtypeStruct((heads, slots, 1), jnp.float32),
+            jax.ShapeDtypeStruct((heads, slots, 1), jnp.float32),
+        ),
+        grid_spec=pltpu.PrefetchScalarGridSpec(
+            num_scalar_prefetch=1,
+            grid=(heads, nq),
+            in_specs=[
+                pl.BlockSpec((1, tq, width), lambda h, i, n: (h, i, 0)),
+                pl.BlockSpec((1, slots, width), lambda h, i, n: (h, 0, 0)),
+                pl.BlockSpec((1, slots, width), lambda h, i, n: (h, 0, 0)),
+            ],
+            out_specs=[
+                pl.BlockSpec((1, tq, width), lambda h, i, n: (h, i, 0)),
+                pl.BlockSpec((1, tq, width), lambda h, i, n: (h, i, 0)),
+                pl.BlockSpec((1, tq, 1), lambda h, i, n: (h, i, 0)),
+                pl.BlockSpec((1, tq, 1), lambda h, i, n: (h, i, 0)),
+            ],
+            scratch_shapes=[pltpu.VMEM((slots // tk, tq, tk), jnp.float32)],
+        ),
+        compiler_params=pltpu.CompilerParams(dimension_semantics=("arbitrary", "arbitrary")),
+        cost_estimate=pl.CostEstimate(
+            flops=2 * heads * slots * slots * width, transcendentals=heads * slots * slots,
+            bytes_accessed=4 * heads * slots * width * 2),
+    )(length.reshape(1), q, k, v)
+
+
+def _bwd_kernel(len_ref, q_ref, k_ref, v_ref, g_ref, m_ref, il_ref, d_ref,
+                dq_ref, dk_ref, dv_ref, dq_scr, *, tq, tk, scale):
+    length = len_ref[0]
+    slots = q_ref.shape[1]
+    nq = slots // tq
+    n_kb = (length + tk - 1) // tk
+    dq_scr[...] = jnp.zeros(dq_scr.shape, jnp.float32)
+    dk_ref[...] = jnp.zeros(dk_ref.shape, jnp.float32)
+    dv_ref[...] = jnp.zeros(dv_ref.shape, jnp.float32)
+
+    def key_block(kb, _):
+        kstart = pl.multiple_of(kb * tk, tk)
+        k = k_ref[0, pl.ds(kstart, tk), :]
+        v = v_ref[0, pl.ds(kstart, tk), :]
+        first_qb = (kb * tk) // tq
+
+        def query_block(qb, carry):
+            dk_acc, dv_acc = carry
+            qstart = pl.multiple_of(qb * tq, tq)
+            q = q_ref[0, pl.ds(qstart, tq), :]
+            g = g_ref[0, pl.ds(qstart, tq), :]
+            s = lax.dot_general(q, k, (((1,), (1,)), ((), ())), preferred_element_type=jnp.float32) * scale
+            s = _mask(s, qb * tq, kb * tk, length)
+            p = jnp.exp(s - m_ref[0, pl.ds(qstart, tq), :]) * il_ref[0, pl.ds(qstart, tq), :]
+            dp = lax.dot_general(g, v, (((1,), (1,)), ((), ())), preferred_element_type=jnp.float32)
+            ds = (p * (dp - d_ref[0, pl.ds(qstart, tq), :])).astype(jnp.bfloat16)
+            dv_acc = dv_acc + lax.dot_general(p.astype(jnp.bfloat16), g, (((0,), (0,)), ((), ())),
+                                              preferred_element_type=jnp.float32)
+            dk_acc = dk_acc + lax.dot_general(ds, q, (((0,), (0,)), ((), ())),
+                                              preferred_element_type=jnp.float32)
+            dq_scr[pl.ds(qstart, tq), :] += jnp.dot(ds, k, preferred_element_type=jnp.float32)
+            return dk_acc, dv_acc
+
+        zero = jnp.zeros((tk, k_ref.shape[2]), jnp.float32)
+        dk_acc, dv_acc = lax.fori_loop(first_qb, nq, query_block, (zero, zero))
+        dk_ref[0, pl.ds(kstart, tk), :] = dk_acc * scale
+        dv_ref[0, pl.ds(kstart, tk), :] = dv_acc
+        return 0
+
+    lax.fori_loop(0, n_kb, key_block, 0)
+    dq_ref[0] = (dq_scr[...] * scale).astype(dq_ref.dtype)
+
+
+def attention_bwd(q, k, v, g, m, inv_l, centre, length, *, tq=256, tk=256):
+    heads, slots, width = q.shape
+    kernel = functools.partial(_bwd_kernel, tq=tq, tk=tk, scale=width ** (-0.5))
+    full = pl.BlockSpec((1, slots, width), lambda h, n: (h, 0, 0))
+    col = pl.BlockSpec((1, slots, 1), lambda h, n: (h, 0, 0))
+    return pl.pallas_call(
+        kernel,
+        out_shape=(
+            jax.ShapeDtypeStruct((heads, slots, width), jnp.bfloat16),
+            jax.ShapeDtypeStruct((heads, slots, width), jnp.float32),
+            jax.ShapeDtypeStruct((heads, slots, width), jnp.float32),
+        ),
+        grid_spec=pltpu.PrefetchScalarGridSpec(
+            num_scalar_prefetch=1,
+            grid=(heads,),
+            in_specs=[full, full, full, full, col, col, col],
+            out_specs=[full, full, full],
+            scratch_shapes=[pltpu.VMEM((slots, width), jnp.float32)],
+        ),
+        compiler_params=pltpu.CompilerParams(dimension_semantics=("arbitrary",)),
+        cost_estimate=pl.CostEstimate(
+            flops=5 * heads * slots * slots * width, transcendentals=heads * slots * slots // 2,
+            bytes_accessed=heads * slots * width * 16),
+    )(length.reshape(1), q, k, v, g, m, inv_l, centre)
+
 
 RQ = 6
 RKV = 2
@@ -145,17 +301,6 @@
         )
         return (turned_query, turned_key, basis_value)
 
-    def block_mask(block_start, block_rows, length):
-        query_pos = block_start + jnp.arange(block_rows, dtype=jnp.int32)
-        return (positions[None, :] <= query_pos[:, None]) & (positions[None, :] < length)
-
-    def block_scores(query_block, key_rows, allowed):
-        scores = (
-            jnp.einsum("qhd,khd->hqk", query_block, key_rows, preferred_element_type=jnp.float32)
-            * score_scale
-        )
-        return jnp.where(allowed[None], scores, masked_score)
-
     inputs = tokens.reshape(local_rows, model_width).astype(jnp.float32)
     inv_first = lax.rsqrt(jnp.mean(inputs * inputs, axis=-1, keepdims=True) + norm_eps)
     normed = (inputs * inv_first * attention_gain).astype(jnp.bfloat16)
@@ -182,36 +327,14 @@
     query_all = combine(head_query, turned_query, RQ)
     key_all = combine(head_key, turned_key, RKV)
     value_all = combine(head_value, basis_value, RKV)
-    sequence_index = 0
-    query_rows = query_all[:, sequence_index]
-    key_rows = key_all[:, sequence_index]
-    value_rows = value_all[:, sequence_index]
-    length = lengths[sequence_index]
-    row_count = query_rows.shape[0]
-    heads_count = query_rows.shape[1]
-    block_rows = min(512, row_count)
-    block_count = row_count // block_rows
-
-    def one_block(block_index):
-        block_start = block_index * block_rows
-        query_block = row_slice(query_rows, block_start, block_rows)
-        scores = block_scores(
-            query_block, key_rows, block_mask(0 + block_start, block_rows, length)
-        )
-        maxima = jnp.max(scores, axis=-1, keepdims=True)
-        raised = jnp.exp(scores - maxima)
-        totals = jnp.sum(raised, axis=-1, keepdims=True)
-        probs_low = (raised / totals).astype(jnp.bfloat16)
-        out_block = jnp.einsum(
-            "hqk,khd->qhd", probs_low, value_rows, preferred_element_type=jnp.float32
-        ).astype(jnp.bfloat16)
-        return (out_block, (maxima + jnp.log(totals))[..., 0])
-
-    out_blocks, log_sums = lax.map(one_block, jnp.arange(block_count))
-    out_rows, log_sums = (out_blocks.reshape(row_count, heads_count, head_width), log_sums)
-    attended = [out_rows]
-    log_sum_list = [log_sums]
-    mixed_heads = jnp.stack(attended, axis=1).reshape(full_rows, heads_here * head_width)
+    length = lengths[0]
+    query_heads_major = query_all[:, 0].transpose(1, 0, 2)
+    key_heads_major = key_all[:, 0].transpose(1, 0, 2)
+    value_heads_major = value_all[:, 0].transpose(1, 0, 2)
+    out_heads, out_full, row_max, row_inv = attention_fwd(
+        query_heads_major, key_heads_major, value_heads_major, length
+    )
+    mixed_heads = out_heads.transpose(1, 0, 2).reshape(full_rows, heads_here * head_width)
     attention_out = lax.psum_scatter(
         matmul(
             row_slice(mixed_heads, jnp.int32(0), local_rows * lax.axis_size("head")), output_weight
@@ -282,70 +405,15 @@
         .astype(jnp.bfloat16)
         .reshape(all_slots, sequences, heads_here, head_width)
     )
-    head_query, head_key, head_value, turned_query, turned_key, basis_value = full_factors()
-    query_all = combine(head_query, turned_query, RQ)
-    key_all = combine(head_key, turned_key, RKV)
-    value_all = combine(head_value, basis_value, RKV)
-    sequence_index = 0
-    attend_query_rows = query_all[:, sequence_index]
-    attend_key_rows = key_all[:, sequence_index]
-    attend_value_rows = value_all[:, sequence_index]
-    grad_rows = heads_grad[:, sequence_index]
-    log_sums = log_sum_list[sequence_index]
-    attend_length = lengths[sequence_index]
-    row_count = attend_query_rows.shape[0]
-    heads_count = attend_query_rows.shape[1]
-    attend_block_rows = min(512, row_count)
-    block_count = row_count // attend_block_rows
-
-    def one_block(carried, block_index):
-        key_grad, value_grad = carried
-        block_start = block_index * attend_block_rows
-        query_block = row_slice(attend_query_rows, block_start, attend_block_rows)
-        grad_block = row_slice(grad_rows, block_start, attend_block_rows)
-        allowed = block_mask(0 + block_start, attend_block_rows, attend_length)
-        scores = block_scores(query_block, attend_key_rows, allowed)
-        probabilities = jnp.where(
-            allowed[None], jnp.exp(scores - log_sums[block_index][..., None]), 0.0
-        )
-        prob_grad = jnp.einsum(
-            "qhd,khd->hqk", grad_block, attend_value_rows, preferred_element_type=jnp.float32
-        )
-        centre = jnp.sum(probabilities * prob_grad, axis=-1, keepdims=True)
-        score_grad = (probabilities * (prob_grad - centre)).astype(jnp.bfloat16)
-        query_grad = (
-            jnp.einsum(
-                "hqk,khd->qhd", score_grad, attend_key_rows, preferred_element_type=jnp.float32
-            )
-            * score_scale
-        ).astype(jnp.bfloat16)
-        key_grad = (
-            key_grad
-            + jnp.einsum(
-                "hqk,qhd->khd", score_grad, query_block, preferred_element_type=jnp.float32
-            )
-            * score_scale
-        )
-        value_grad = value_grad + jnp.einsum(
-            "hqk,qhd->khd",
-            probabilities.astype(jnp.bfloat16),
-            grad_block,
-            preferred_element_type=jnp.float32,
-        )
-        return ((key_grad, value_grad), query_grad)
-
-    zero_block = jnp.zeros(attend_key_rows.shape, jnp.float32)
-    (key_grad, value_grad), query_blocks = lax.scan(
-        one_block, (zero_block, zero_block), jnp.arange(block_count)
-    )
-    query_grad, key_grad, value_grad = (
-        query_blocks.reshape(row_count, heads_count, head_width),
-        key_grad,
-        value_grad,
-    )
-    query_grads = [query_grad]
-    key_grads = [key_grad]
-    value_grads = [value_grad]
+    grad_heads_major = heads_grad[:, 0].transpose(1, 0, 2)
+    centre = jnp.sum(grad_heads_major.astype(jnp.float32) * out_full, axis=-1, keepdims=True)
+    query_grad, key_grad, value_grad = attention_bwd(
+        query_heads_major, key_heads_major, value_heads_major, grad_heads_major,
+        row_max, row_inv, centre, length,
+    )
+    query_grads = [query_grad.transpose(1, 0, 2)]
+    key_grads = [key_grad.transpose(1, 0, 2)]
+    value_grads = [value_grad.transpose(1, 0, 2)]
     query_grad_all = jnp.stack(query_grads, axis=1).astype(jnp.float32)
     key_grad_all = jnp.stack(key_grads, axis=1)
     value_grad_all = jnp.stack(value_grads, axis=1)

time: 1730 us -> 1560 us (0.902)
  matrix products: 575 us -> 146 us
  waiting for transfers between devices: 670 us -> 948 us
  Pallas kernels: 0 us -> 101 us
  other arithmetic: 267 us -> 175 us
    dot_general x28 -> x0, matrix products: 431 us -> none  [the longest x8 167 us: block_scores(): jnp.einsum('qhd,khd->hqk', query_block, key_rows, preferred_element_type=...]
    psum x1, waiting for transfers between devices: 17 us -> 149 us  [per_device(): lax.psum(grad_key_part.astype(jnp.bfloat16), 'dp').astype(jnp.float32)]
    reduce_scatter x1, waiting for transfers between devices: 54.5 us -> 182 us  [per_device(): lax.psum_scatter(matmul(row_slice(mixed_heads, jnp.int32(0), local_rows *...]
    convert_element_type x4 -> x0, other arithmetic: 110 us -> none  [one_block(): score_grad = (probabilities * (prob_grad - centre)).astype(jnp.bfloat16)]
    pallas_call x0 -> x2, Pallas kernels: none -> 101 us  [the longest x1 58.4 us: attention_fwd(): pl.pallas_call(kernel, out_shape=(jax.ShapeDtypeStruct((heads, slots, wid...]
    reduce_sum x4 -> x1, other arithmetic: 60.2 us -> 6.81 us  [per_device(): jnp.sum(grad_heads_major.astype(jnp.float32) * out_full, axis=-1, keepdim...]
    reduce_sum x3, other arithmetic: 17.3 us -> 57.5 us  [factor_grad(): jnp.sum(grad_rows * turned_part[:, :, rank_index][:, :, None, :], axis=-1)]
    unnamed x150 -> x174, local copies, waits for them, and re-layouts: 31.3 us -> 56.2 us
  transfers between devices with their start and end apart: 11 -> 11, of which waited for: 11 -> 11; matrix products, arithmetic and copies ran while one was open for 12% -> 11% of each run, Pallas kernels for 0% -> 0%
where the time goes in v1:
time: 1560 us; the launch traced here: 1540 us
  waiting for transfers between devices  948 us (61%)
  other arithmetic  175 us (11%)
  matrix products  146 us (9%)
  local copies, waits for them, and re-layouts  118 us (8%)
  Pallas kernels  101 us (6%)
  blocking collectives  39.6 us (3%)
  between operations  15.7 us (1%)
    psum x1, waiting for transfers between devices, per_device(): lax.psum(grad_query_part.astype(jnp.bfloat16), 'dp').astype(jnp.float32)  195 us
    reduce_scatter x1, waiting for transfers between devices, per_device(): lax.psum_scatter(matmul(row_slice(mixed_heads, jnp.int32(0), local_rows *...  182 us
    psum x1, waiting for transfers between devices, per_device(): lax.psum(grad_key_part.astype(jnp.bfloat16), 'dp').astype(jnp.float32)  149 us
    dot_general x18, matrix products, matmul(): jnp.dot(first_operand, second_operand, preferred_element_type=jnp.float32)  146 us
    psum x1, waiting for transfers between devices, per_device(): lax.psum((grad_basis[:, :basis_query_cols], grad_basis[:, basis_query_col...  87.5 us
    reduce_scatter x1, waiting for transfers between devices, per_device(): lax.psum_scatter(jnp.concatenate([matmul(head_part, head_cat.T), basis_pa...  70.5 us
    pallas_call x1, Pallas kernels, attention_fwd(): pl.pallas_call(kernel, out_shape=(jax.ShapeDtypeStruct((heads, slots, wid...  58.4 us
    reduce_sum x3, other arithmetic, factor_grad(): jnp.sum(grad_rows * turned_part[:, :, rank_index][:, :, None, :], axis=-1)  57.5 us
  transfers between devices with their start and end apart: 11, of which 11 were waited for; matrix products, arithmetic and copies ran while one was open for 11% of the time, Pallas kernels for 0%

profile of v1, /device:TPU:0, one launch (start us, length us, event | category | flops | bytes accessed | tf_op | source)
XLA Modules:
  0.0 1544.0 jit_solution(12074051134045676792)
XLA Ops:
  26.0 47.8 %all-gather.7.cloned.1.call-done = bf16[2048,1,1024]{2,0,1:T(8,128)(2,1)} async-done(((bf16[1024,1,1024]{2,0,1:T(8,128)(2,1)}), bf16[2048,1,1024]{2,0,1:T(8,128)(2,1)}) %all-gather.7.cloned.1.call-update) | async-done | bytes 4194320 | tf_op jit(solution)/shard_map/all_gather | solution.py:313
  138.2 6.5 multiply_convert_fusion.4.k_ref
  151.0 15.1 multiply_convert_fusion.5.q_ref
  166.1 58.4 %shard_map.254 = (bf16[8,2048,64]{2,1,0:T(8,128)(2,1)}, f32[8,2048,64]{2,1,0:T(8,128)}, f32[8,2048,1]{2,1,0:T(8,128)}, f32[8,2048,1]{2,1,0:T(8,128)}) custom-call(s32[1]{0:T(128)S(6)} %copy.163.len_ref, bf16[8,2048,64]{2,1,0:T(8,128)(2,1)} %multiply_convert_fusion.5.q_ref, bf16[8,2048,64]{2,1,0:T(8,128)(2,1)} %multiply_convert_fusion.4.k_ref, ...), custom_call_target="tpu_custom_call" | custom-call | flops 4294967296 | bytes 8388608 | tf_op jit(solution)/shard_map/pallas_call | solution.py:62
  235.6 181.5 %reduce-scatter.5.cloned.1.call-done = bf16[1024,1024]{1,0:T(8,128)(2,1)} async-done(((bf16[2048,1024]{1,0:T(8,128)(2,1)}), bf16[1024,1024]{1,0:T(8,128)(2,1)}) %reduce-scatter.5.cloned.1.call-update) | async-done | bytes 2097168 | tf_op jit(solution)/shard_map/reduce_scatter | solution.py:338
  423.4 56.3 %all-gather.11.cloned.1.call-done = bf16[2048,1024]{1,0:T(8,128)(2,1)} async-done(((bf16[1024,1024]{1,0:T(8,128)(2,1)}), bf16[2048,1024]{1,0:T(8,128)(2,1)}) %all-gather.11.cloned.1.call-update) | async-done | bytes 4194320 | tf_op jit(solution)/shard_map/all_gather | solution.py:350
  479.6 12.4 fusion.98
  492.0 9.3 fusion.97
  501.3 36.5 %all-gather.9.cloned.1.call-done = bf16[2048,1,1024]{2,0,1:T(8,128)(2,1)} async-done(((bf16[1024,1,1024]{2,0,1:T(8,128)(2,1)}), bf16[2048,1,1024]{2,0,1:T(8,128)(2,1)}) %all-gather.9.cloned.1.call-update) | async-done | bytes 4194320 | tf_op jit(solution)/shard_map/all_gather | solution.py:368
  537.8 20.5 %multiply_convert_fusion = (bf16[2048,1408]{1,0:T(8,128)(2,1)}, bf16[2048,1408]{1,0:T(8,128)(2,1)}, bf16[2048,1408]{1,0:T(8,128)(2,1)}) fusion(f32[2048,1408]{1,0:T(8,128)} %fusion.97, f32[2048,1408]{1,0:T(8,128)} %fusion.98, bf16[1408,1024]{1,0:T(8,128)(2,1)S(1)} %copy-done, bf16[2048,1,1024]{2,0,1:T(8,128)(2,1)} %all-gather.9.cloned.1.call-done), kind=kOutput, calls=%fused_computation | convolution fusion | flops 5951717376 | bytes 47448064 | tf_op jit(solution)/shard_map/dot_general | solution.py:208
  558.3 9.7 fusion.99
  568.0 8.6 add_convert_fusion
  576.7 54.5 %reduce-scatter.9.cloned.1.call-done = bf16[1024,1024]{1,0:T(8,128)(2,1)} async-done(((bf16[2048,1024]{1,0:T(8,128)(2,1)}), bf16[1024,1024]{1,0:T(8,128)(2,1)}) %reduce-scatter.9.cloned.1.call-update) | async-done | bytes 2097168 | tf_op jit(solution)/shard_map/reduce_scatter | solution.py:380
  640.6 11.5 convolution_convert_fusion
  652.1 11.3 convolution_convert_fusion.1
  663.4 7.6 fusion.54
  670.9 26.5 %all-gather.13.cloned.1.call-done = bf16[2048,1024]{1,0:T(8,128)(2,1)} async-done(((bf16[1024,1024]{1,0:T(8,128)(2,1)}), bf16[2048,1024]{1,0:T(8,128)(2,1)}) %all-gather.13.cloned.1.call-update) | async-done | bytes 4194320 | tf_op jit(solution)/shard_map/all_gather | solution.py:399
  708.7 6.8 multiply_reduce_fusion
  720.1 42.5 %shard_map.255 = (bf16[8,2048,64]{2,1,0:T(8,128)(2,1)}, f32[8,2048,64]{2,1,0:T(8,128)}, f32[8,2048,64]{2,1,0:T(8,128)}) custom-call(s32[1]{0:T(128)S(6)} %copy.163.len_ref, bf16[8,2048,64]{2,1,0:T(8,128)(2,1)} %multiply_convert_fusion.5.q_ref, bf16[8,2048,64]{2,1,0:T(8,128)(2,1)} %multiply_convert_fusion.4.k_ref, ...), custom_call_target="tpu_custom_call" | custom-call | flops 10737418240 | bytes 16777216 | tf_op jit(solution)/shard_map/pallas_call | solution.py:141
  762.7 32.8 %fusion.13 = (f32[2048,8]{0,1:T(8,128)S(1)}, f32[2048,64]{1,0:T(8,128)}, f32[2048,64]{1,0:T(8,128)}, f32[2048,64]{1,0:T(8,128)}, f32[2048,64]{1,0:T(8,128)}, /*i...) fusion(bf16[8,2048,64]{2,1,0:T(8,128)(2,1)} %get-tuple-element., ...), kind=kLoop, calls=%fused_computation.37 | loop fusion | flops 25329664 | bytes 9175040 | tf_op jit(solution)/shard_map/reduce_sum | solution.py:227
  795.6 12.3 fusion.4
  808.7 12.3 fusion
  887.7 11.0 convolution_convert_fusion.2
  898.8 148.9 %all-reduce.10.cloned.1.call-done = (bf16[1024,16]{0,1:T(8,128)(2,1)}, bf16[1024,16]{0,1:T(8,128)(2,1)}) async-done(((bf16[1024,16]{0,1:T(8,128)(2,1)}, bf16[1024,16]{0,1:T(8,128)(2,1)}), (bf16[1024,16]{0,1:T(8,128)(2,1)}, bf16[1024,16]{0,1:T(8,128)(2,1)})) %all-reduce.10.cloned.1.call-update) | async-done | bytes 65552 | tf_op jit(solution)/shard_map/psum | solution.py:469
  1050.5 195.1 %all-reduce.12.cloned.1.call-done = (bf16[1024,48]{0,1:T(8,128)(2,1)}, bf16[512,1024]{1,0:T(8,128)(2,1)}, bf16[1024,1408]{1,0:T(8,128)(2,1)}, bf16[1024,1408]{1,0:T(8,128)(2,1)}, bf16[1408,1024]{1,0:T(8,128)(2,1)}) async-done(((bf16[1024,48]{0,1:T(8,128)(2,1)}, bf16[512,1024]{1,0:T(8,128)(2,1)}, bf16[1024,1408]{1,0:T(8,128)(2,1)}, bf16[1024,1408]{1,0:T(8,128)(2,1)}, bf16[1408,1024]{1,0:T(8,128)(2,1)}), ...) | async-done | bytes 9797648 | tf_op jit(solution)/shard_map/psum | solution.py:468
  1260.2 70.5 %reduce-scatter.11.cloned.1.call-done = bf16[1024,1664]{1,0:T(8,128)(2,1)} async-done(((bf16[2048,1664]{1,0:T(8,128)(2,1)}), bf16[1024,1664]{1,0:T(8,128)(2,1)}) %reduce-scatter.11.cloned.1.call-update) | async-done | bytes 3407888 | tf_op jit(solution)/shard_map/reduce_scatter | solution.py:451
  1337.0 8.1 fusion.39
  1345.1 42.1 %reduce-scatter.7.cloned.1.call-done = bf16[1024,1024]{1,0:T(8,128)(2,1)} async-done(((bf16[2048,1024]{1,0:T(8,128)(2,1)}), bf16[1024,1024]{1,0:T(8,128)(2,1)}) %reduce-scatter.7.cloned.1.call-update) | async-done | bytes 2097168 | tf_op jit(solution)/shard_map/reduce_scatter | solution.py:357
  1387.3 8.7 fusion.36
  1396.0 8.5 copy.104
  1404.5 39.6 %all-reduce = (f32[1024]{0:T(1024)}, f32[1024]{0:T(1024)}) all-reduce(f32[1024]{0:T(1024)S(1)} %get-tuple-element.80, f32[1024]{0:T(1024)S(1)} %copy-done.63), channel_id=1, replica_groups=mesh['dp'=16,'head'=2] {'dp','head'}, use_global_device_ids=true, to_apply=%region_30.0 | all-reduce | flops 2048 | bytes 16384 | tf_op jit(solution)/shard_map/psum | solution.py:476
  1444.1 87.5 %all-reduce.8.cloned.1.call-done = (f32[1024,384]{1,0:T(8,128)}, f32[1024,128]{1,0:T(8,128)}, f32[1024,128]{1,0:T(8,128)}) async-done(((f32[1024,384]{1,0:T(8,128)}, f32[1024,128]{1,0:T(8,128)}, f32[1024,128]{1,0:T(8,128)}), (f32[1024,384]{1,0:T(8,128)}, f32[1024,128]{1,0:T(8,128)}, f32[1024,128]{1,0:T(8,128)})) %all-reduce.8.cloned.1.call-update) | async-done | bytes 2621456 | tf_op jit(solution)/shard_map/psum | solution.py:476
  (286 shorter events, 227.6 us)
Async XLA Ops:
  7.2 530.6 %copy-start = (bf16[1408,1024]{1,0:T(8,128)(2,1)S(1)}, bf16[1408,1024]{1,0:T(8,128)(2,1)}, u32[]{:S(2)}) copy-start(bf16[1408,1024]{1,0:T(8,128)(2,1)} %param.29) | copy-start | bytes 8650756
  7.2 66.6 %all-gather.7.cloned.1.call-start = ((), (), s32[]{:S(2)}) async-start(), calls=%async_computation.4 | async-start | bytes 6291456 | tf_op jit(solution)/shard_map/all_gather | solution.py:313
  14.2 402.9 %reduce-scatter.5.cloned.1.call-start = ((), (), s32[]{:S(2)}) async-start(), calls=%async_computation.5 | async-start | bytes 6291456 | tf_op jit(solution)/shard_map/reduce_scatter | solution.py:338
  138.1 12.9 copy-start.19
  138.1 12.8 copy-start.20
  138.1 12.8 copy-start.21
  138.1 12.8 copy-start.22
  138.1 12.8 copy-start.23
  138.1 12.8 copy-start.24
  235.5 184.7 %copy-start.58 = (f32[1024]{0:T(1024)S(1)}, f32[1024]{0:T(1024)}, u32[]{:S(2)}) copy-start(f32[1024]{0:T(1024)} %param.26) | copy-start | bytes 12292
  235.6 244.1 %all-gather.11.cloned.1.call-start = ((), (), s32[]{:S(2)}) async-start(), calls=%async_computation.10 | async-start | bytes 6291456 | tf_op jit(solution)/shard_map/all_gather | solution.py:350
  422.7 115.0 %all-gather.9.cloned.1.call-start = ((), (), s32[]{:S(2)}) async-start(), calls=%async_computation.7 | async-start | bytes 6291456 | tf_op jit(solution)/shard_map/all_gather | solution.py:368
  423.3 207.8 %reduce-scatter.9.cloned.1.call-start = ((), (), s32[]{:S(2)}) async-start(), calls=%async_computation.8 | async-start | bytes 6291456 | tf_op jit(solution)/shard_map/reduce_scatter | solution.py:380
  479.6 12.4 copy-start.65
  479.6 12.4 copy-start.68
  576.6 120.8 %all-gather.13.cloned.1.call-start = ((), (), s32[]{:S(2)}) async-start(), calls=%async_computation.11 | async-start | bytes 6291456 | tf_op jit(solution)/shard_map/all_gather | solution.py:399
  640.5 407.2 %all-reduce.10.cloned.1.call-start = ((), (), s32[]{:S(2)}) async-start(), calls=%async_computation.13 | async-start | bytes 131072 | tf_op jit(solution)/shard_map/psum | solution.py:469
  640.5 11.5 copy-start.66
  640.5 22.8 %slice-start.4 = ((s8[5767168]{0:T(1024)(128)(4,1)}), s8[4194304]{0:T(1024)(128)(4,1)S(1)}, s32[]{:S(2)}) async-start(s8[5767168]{0:T(1024)(128)(4,1)} %bitcast.321), calls=%async_computation.19 | async-start | bytes 8388608
  720.1 42.5 %copy-start.46 = (f32[2048,8]{0,1:T(8,128)S(1)}, f32[2048,8]{0,1:T(8,128)}, u32[]{:S(2)}) copy-start(f32[2048,8]{0,1:T(8,128)} %get-tuple-element.153) | copy-start | bytes 196612
  720.1 42.5 %copy-start.47 = (f32[2048,8]{0,1:T(8,128)S(1)}, f32[2048,8]{0,1:T(8,128)}, u32[]{:S(2)}) copy-start(f32[2048,8]{0,1:T(8,128)} %get-tuple-element.183) | copy-start | bytes 196612
  762.6 32.9 %copy-start.44 = (f32[2048,8]{0,1:T(8,128)S(1)}, f32[2048,8]{0,1:T(8,128)}, u32[]{:S(2)}) copy-start(f32[2048,8]{0,1:T(8,128)} %get-tuple-element.163) | copy-start | bytes 196612
  762.7 32.9 %copy-start.45 = (f32[2048,8]{0,1:T(8,128)S(1)}, f32[2048,8]{0,1:T(8,128)}, u32[]{:S(2)}) copy-start(f32[2048,8]{0,1:T(8,128)} %get-tuple-element.185) | copy-start | bytes 196612
  795.5 13.1 copy-start.42
  795.5 13.1 copy-start.43
  836.8 408.8 %all-reduce.12.cloned.1.call-start = ((), (), s32[]{:S(2)}) async-start(), calls=%async_computation.14 | async-start | bytes 19595264 | tf_op jit(solution)/shard_map/psum | solution.py:468
  858.8 471.9 %reduce-scatter.11.cloned.1.call-start = ((), (), s32[]{:S(2)}) async-start(), calls=%async_computation.9 | async-start | bytes 10223616 | tf_op jit(solution)/shard_map/reduce_scatter | solution.py:451
  887.5 499.8 %reduce-scatter.7.cloned.1.call-start = ((), (), s32[]{:S(2)}) async-start(), calls=%async_computation.6 | async-start | bytes 6291456 | tf_op jit(solution)/shard_map/reduce_scatter | solution.py:357
  898.7 632.9 %all-reduce.8.cloned.1.call-start = ((), (), s32[]{:S(2)}) async-start(), calls=%async_computation.12 | async-start | bytes 5242880 | tf_op jit(solution)/shard_map/psum | solution.py:476
  1256.9 73.8 %copy-start.60 = (f32[1024]{0:T(1024)S(1)}, f32[1024]{0:T(1024)}, u32[]{:S(2)}) copy-start(f32[1024]{0:T(1024)} %copy-done.59) | copy-start | bytes 12292
  1256.9 73.8 %copy-start.64 = (f32[1024]{0:T(1024)S(1)}, f32[1024]{0:T(1024)}, u32[]{:S(2)}) copy-start(f32[1024]{0:T(1024)} %param.18) | copy-start | bytes 12292
  1337.0 50.3 %copy-start.62 = (f32[1024]{0:T(1024)S(1)}, f32[1024]{0:T(1024)}, u32[]{:S(2)}) copy-start(f32[1024]{0:T(1024)} %get-tuple-element.171) | copy-start | bytes 12292
  (56 other events, 320.2 us)
Sparse Core Ops, SparseCore 0:
  14.3 59.4 all-gather.6
  235.7 181.4 reduce-scatter.4
  422.8 56.7 all-gather.10
  481.0 56.7 all-gather.8
  576.7 54.3 reduce-scatter.8
  640.6 56.7 all-gather.12
  836.9 210.7 all-reduce.9
  1053.2 192.3 all-reduce.11
  1247.9 82.8 reduce-scatter.10
  1332.9 54.3 reduce-scatter.6
  1394.2 137.3 all-reduce.7
